TPU v7x, 256 devices: a whole 4x4x8 slice. The times are simulated.
256 devices in a mesh: section: 2 (over x_hi), ctx: 32 (over z, x_lo, core), mp: 4 (over y).
Axes of the slice: x: 4 (x_hi: 2, x_lo: 2; x = x_hi * 2 + x_lo), y: 4, z: 8, core: 2. Of those that a mesh axis runs over, the one named last changes fastest.
Arguments:
- queries: bfloat16 [2, 8192, 4096], P('section', 'ctx', 'mp'), may hold values from -130 to 130
- keys: bfloat16 [2, 8192, 512], P('section', 'ctx', 'mp'), may hold values from -4.5 to 4.5
- values: bfloat16 [2, 8192, 512], P('section', 'ctx', 'mp'), may hold values from -6 to 6
- doc_lengths: int32 [2, 16], P('section'), may hold values from 1 to 4096, 8192 in all within a row
Outputs:
- attended: bfloat16 [2, 8192, 4096], P('section', ('ctx', 'mp'))
- passed: bfloat16 [2, 8192, 4096], P('section', ('ctx', 'mp'))
All inputs are finite; a program needn't handle non-finite values.
Results may differ from a plain program's by a relative error of at most 0.004.
Values may be sent and summed in bfloat16 or wider, within the bound.
No kernel may reach another device: no remote copies, remote signals or barrier semaphores. Data moves between devices by JAX's collectives and lax.ppermute only.
A program may use at most 192 MiB of HBM per device.

v0:
```python
import math

import jax
import jax.numpy as jnp
from jax import lax
from jax.sharding import PartitionSpec as P

DH = 128
DOCS = 16


def from_behind(block, axis, distance):
    devices = range(lax.axis_size(axis))
    route = [((i - distance) % len(devices), i) for i in devices]
    return lax.ppermute(block, axis, route)


def doc_of(positions, ends):
    return jnp.sum((positions[:, None] >= ends[None, :]).astype(jnp.int32), axis=1)


def body(queries, keys, values, doc_lengths):
    query_rows = queries[0]
    key_rows = keys[0]
    value_rows = values[0]
    lengths = doc_lengths[0]
    rows = query_rows.shape[0]
    kv_heads = key_rows.shape[1] // DH
    heads = query_rows.shape[1] // DH
    group = heads // kv_heads
    cycle = lax.axis_size("ctx")
    base_len = rows * cycle // 16
    position = lax.axis_index("ctx")
    first = position * rows
    ends = jnp.cumsum(lengths)
    query_pos = first + jnp.arange(rows, dtype=jnp.int32)
    query_doc = doc_of(query_pos, ends)
    lookup = query_doc[:, None] == jnp.arange(DOCS, dtype=jnp.int32)[None, :]
    query_len = jnp.sum(jnp.where(lookup, lengths[None, :], 0), axis=1).astype(jnp.float32)
    factor = jnp.maximum(1.0, jnp.log(query_len) / math.log(float(base_len))) * (
        1.0 / math.sqrt(DH)
    )
    query_heads = query_rows.reshape(rows, kv_heads, group, DH)
    key_piece = lax.all_gather(key_rows, "ctx", axis=0, tiled=True)
    value_piece = lax.all_gather(value_rows, "ctx", axis=0, tiled=True)
    top = jnp.full((kv_heads, group, rows), -1e30, jnp.float32)
    count = key_piece.shape[0]
    key_pos = jnp.arange(count, dtype=jnp.int32)
    key_doc = doc_of(key_pos, ends)
    score = jnp.einsum(
        "qhgd,khd->hgqk",
        query_heads,
        key_piece.reshape(count, kv_heads, DH),
        preferred_element_type=jnp.float32,
    )
    score = score * factor[None, None, :, None]
    allowed = (
        (query_doc[:, None] == key_doc[None, :])
        & (key_pos[None, :] <= query_pos[:, None])
        & (key_pos[None, :] >= 0)
    )
    score = jnp.where(allowed[None, None], score, -1e30)
    new_top = jnp.maximum(top, jnp.max(score, axis=-1))
    weight = jnp.where(allowed[None, None], jnp.exp(score - new_top[..., None]), 0.0)
    total = jnp.sum(weight, axis=-1)
    update = jnp.einsum(
        "hgqk,khd->qhgd",
        weight.astype(jnp.bfloat16),
        value_piece.reshape(count, kv_heads, DH),
        preferred_element_type=jnp.float32,
    )
    summed = update
    top, total, summed = (new_top, total, summed)
    result = summed / jnp.transpose(total, (2, 0, 1))[..., None]
    result = result.astype(jnp.bfloat16).reshape(rows, heads * DH)
    own = lax.all_to_all(result, "mp", split_axis=0, concat_axis=1, tiled=True)
    moved = from_behind(own, "section", 1)
    return (own[None], moved[None])


def solution(mesh):
    return jax.shard_map(
        body,
        mesh=mesh,
        in_specs=(
            P("section", "ctx", "mp"),
            P("section", "ctx", "mp"),
            P("section", "ctx", "mp"),
            P("section", None),
        ),
        out_specs=(P("section", ("ctx", "mp"), None), P("section", ("ctx", "mp"), None)),
        check_vma=False,
    )
```

profile of v0, /device:TPU:128, one launch (start us, length us, event | category | flops | bytes accessed | tf_op | source)
XLA Modules:
  0.0 206.4 jit_solution(6878893363365230713)
XLA Ops:
  7.2 0.0 all-gather.5.cloned.1.call-start
  7.2 0.7 all-gather.5.cloned.1.call-update
  7.9 0.0 all-gather.7.cloned.1.call-start
  7.9 0.7 all-gather.7.cloned.1.call-update
  8.7 0.7 copy.19
  9.4 0.1 reduce.2
  9.5 0.2 convert_reduce_fusion
  9.7 0.1 convert_reduce_fusion.1
  9.8 3.7 %fusion.7 = pred[256,8192]{0,1:T(8,128)(4,1)S(1)} fusion(s32[256]{0:T(256)S(1)} %iota_add_fusion, s32[256]{0:T(256)S(1)} %convert_reduce_fusion.1, s32[8192]{0:T(1024)S(1)} %convert_reduce_fusion), kind=kLoop, calls=%fused_computation.10 | loop fusion | flops 6291456 | bytes 2131968 | tf_op jit(solution)/shard_map/and | solution.py:58
  13.5 0.7 select_reduce_fusion
  14.3 1.1 copy.27
  15.4 58.7 %all-gather.5.cloned.1.call-done = bf16[1,8192,128]{2,1,0:T(8,128)(2,1)} async-done(((bf16[1,256,128]{2,1,0:T(8,128)(2,1)}), bf16[1,8192,128]{2,1,0:T(8,128)(2,1)}) %all-gather.5.cloned.1.call-update) | async-done | bytes 2097168 | tf_op jit(solution)/shard_map/all_gather | solution.py:44
  74.2 24.9 %fusion = (f32[8,256]{1,0:T(8,128)S(1)}, f32[8192,256,8]{1,0,2:T(8,128)}) fusion(f32[256]{0:T(256)S(1)} %maximum_multiply_fusion, pred[256,8192]{0,1:T(8,128)(4,1)S(1)} %fusion.7, bf16[256,8,128]{2,1,0:T(8,128)(2,1)S(1)} %bitcast.88, bf16[1,8192,128]{2,1,0:T(8,128)(2,1)} %all-gather.5.cloned.1.call-done), kind=kOutput, calls=%fused_computation.3 | convolution fusion | flops 4345296896 | bytes 71836672 | tf_op jit(solution)/shard_map/qhgd,khd->hgqk/dot_general | solution.py:50
  99.1 22.0 %fusion.1 = f32[8,256]{1,0:T(8,128)S(1)} fusion(f32[8192,256,8]{1,0,2:T(8,128)} %get-tuple-element.3, f32[8,256]{1,0:T(8,128)S(1)} %broadcast_maximum_fusion, f32[256]{0:T(256)S(1)} %maximum_multiply_fusion, pred[256,8192]{0,1:T(8,128)(4,1)S(1)} %fusion.7), kind=kLoop, calls=%fused_computation.4 | loop fusion | flops 83884032 | bytes 69223424 | tf_op jit(solution)/shard_map/reduce_sum | solution.py:65
  121.0 19.0 %all-gather.7.cloned.1.call-done = bf16[1,8192,128]{2,1,0:T(8,128)(2,1)} async-done(((bf16[1,256,128]{2,1,0:T(8,128)(2,1)}), bf16[1,8192,128]{2,1,0:T(8,128)(2,1)}) %all-gather.7.cloned.1.call-update) | async-done | bytes 2097168 | tf_op jit(solution)/shard_map/all_gather | solution.py:45
  140.1 29.6 %divide_convert_fusion = bf16[256,1,8,128]{3,0,2,1:T(8,128)(2,1)S(1)} fusion(bf16[1,8192,128]{2,1,0:T(8,128)(2,1)} %all-gather.7.cloned.1.call-done, f32[8192,256,8]{1,0,2:T(8,128)} %get-tuple-element.3, f32[8,256]{1,0:T(8,128)S(1)} %broadcast_maximum_fusion, f32[256]{0:T(256)S(1)} %maximum_multiply_fusion, pred[256,8192]{0,1:T(8,128)(4,1)S(1)} %fusion.7, ...), kind=kOutput, calls=%fused_computation.15 | convolution fusion | flops 4379377664 | bytes 71844864 | tf_op jit(solution)/shard_map/hgqk,khd->qhgd/dot_general | solution.py:66
  169.7 0.3 copy.22
  170.1 0.2 all_to_all.14
  170.3 13.9 %all_to_all.19 = bf16[4,64,1024]{2,1,0:T(8,128)(2,1)S(1)} all-to-all(bf16[4,64,1024]{2,1,0:T(8,128)(2,1)S(1)} %all_to_all.14), channel_id=1, replica_groups=mesh['section'=2,'ctx'=32,'mp'=4] {'mp'}, dimensions={0} | all-to-all | bytes 1048576 | tf_op jit(solution)/shard_map/all_to_all | solution.py:76
  184.3 3.0 %collective-permute-start = (bf16[64,4096]{1,0:T(8,128)(2,1)S(1)}, bf16[64,4096]{1,0:T(8,128)(2,1)S(1)}, u32[]{:S(2)}, u32[]{:S(2)}) collective-permute-start(bf16[64,4096]{1,0:T(8,128)(2,1)S(1)} %bitcast.87), channel_id=1, source_target_pairs={{128,0},{0,128},{129,1},{1,129},{130,2},{2,130},{131,3},{3,131},{1... | collective-permute-start | bytes 1572872 | tf_op jit(solution)/shard_map/ppermute | solution.py:15
  187.3 0.4 copy.23
  187.7 1.2 broadcast_in_dim.64
  188.8 9.9 %collective-permute-done = bf16[64,4096]{1,0:T(8,128)(2,1)S(1)} collective-permute-done((bf16[64,4096]{1,0:T(8,128)(2,1)S(1)}, bf16[64,4096]{1,0:T(8,128)(2,1)S(1)}, u32[]{:S(2)}, u32[]{:S(2)}) %collective-permute-start) | collective-permute-done | bytes 524320 | tf_op jit(solution)/shard_map/ppermute | solution.py:15
  198.8 0.8 copy.33
  (5 shorter events, 0.1 us)
Async XLA Ops:
  7.2 67.0 %all-gather.5.cloned.1.call-start = ((), (), s32[]{:S(2)}) async-start(), calls=%async_computation.1 | async-start | bytes 2162688 | tf_op jit(solution)/shard_map/all_gather | solution.py:44
  7.9 132.2 %all-gather.7.cloned.1.call-start = ((), (), s32[]{:S(2)}) async-start(), calls=%async_computation.2 | async-start | bytes 2162688 | tf_op jit(solution)/shard_map/all_gather | solution.py:45
  184.3 14.5 %collective-permute-start = (bf16[64,4096]{1,0:T(8,128)(2,1)S(1)}, bf16[64,4096]{1,0:T(8,128)(2,1)S(1)}, u32[]{:S(2)}, u32[]{:S(2)}) collective-permute-start(bf16[64,4096]{1,0:T(8,128)(2,1)S(1)} %bitcast.87), channel_id=1, source_target_pairs={{128,0},{0,128},{129,1},{1,129},{130,2},{2,130},{131,3},{3,131},{1... | collective-permute-start | bytes 1572872 | tf_op jit(solution)/shard_map/ppermute | solution.py:15
Sparse Core Ops, SparseCore 0:
  9.8 64.3 all-gather.4
  76.0 63.9 all-gather.6
where the time goes:
time: 209 us; the launch traced here: 206 us
  waiting for transfers between devices  89.1 us (43%)
  matrix products  54.5 us (26%)
  other arithmetic  26.9 us (13%)
  between operations  14.1 us (7%)
  blocking collectives  13.9 us (7%)
  local copies, waits for them, and re-layouts  4.85 us (2%)
  starting transfers between devices  3.06 us (1%)
    all_gather x1, waiting for transfers between devices, body(): key_piece = lax.all_gather(key_rows, 'ctx', axis=0, tiled=True)  58.7 us
    dot_general x1, matrix products, body(): jnp.einsum('hgqk,khd->qhgd', weight.astype(jnp.bfloat16), value_piece.res...  29.6 us
    dot_general x1, matrix products, body(): jnp.einsum('qhgd,khd->hgqk', query_heads, key_piece.reshape(count, kv_hea...  24.9 us
    reduce_sum x1, other arithmetic, body(): total = jnp.sum(weight, axis=-1)  22 us
    all_gather x1, waiting for transfers between devices, body(): value_piece = lax.all_gather(value_rows, 'ctx', axis=0, tiled=True)  19 us
    all_to_all x1, blocking collectives, body(): own = lax.all_to_all(result, 'mp', split_axis=0, concat_axis=1, tiled=True)  13.9 us
    ppermute x1, waiting for transfers between devices, from_behind(): return lax.ppermute(block, axis, route)  9.94 us
  transfers between devices with their start and end apart: 3, of which 3 were waited for; matrix products, arithmetic and copies ran while one was open for 27% of the time, Pallas kernels for 0%

commit v1 on v0

v1 whole, which is shorter than its diff:
```python
import functools
import math

import jax
import jax.numpy as jnp
from jax import lax
from jax.experimental import pallas as pl
from jax.experimental.pallas import tpu as pltpu
from jax.sharding import PartitionSpec as P

DH = 128
DOCS = 16
MOST = 4096
BK = 512


def from_behind(block, axis, distance):
    devices = range(lax.axis_size(axis))
    route = [((i - distance) % len(devices), i) for i in devices]
    return lax.ppermute(block, axis, route)


def doc_of(positions, ends):
    return jnp.sum((positions[:, None] >= ends[None, :]).astype(jnp.int32), axis=1)


def flash_kernel(bounds_ref, q_ref, kv_ref, qdoc_ref, qpos_ref, fac_ref, kdoc_ref,
                 o_ref, m_sc, l_sc, acc_sc, *, heads, bk, steps):
    j = pl.program_id(0)
    lo = bounds_ref[0]
    hi = bounds_ref[1]

    @pl.when(j == 0)
    def _():
        m_sc[...] = jnp.full(m_sc.shape, -1e30, jnp.float32)
        l_sc[...] = jnp.zeros(l_sc.shape, jnp.float32)
        acc_sc[...] = jnp.zeros(acc_sc.shape, jnp.float32)

    blk = lo + j

    @pl.when(blk <= hi)
    def _():
        k = kv_ref[:, :DH]
        v = kv_ref[:, DH:]
        kpos = blk * bk + lax.broadcasted_iota(jnp.int32, (1, bk), 1)
        allowed = (qdoc_ref[...] == kdoc_ref[...]) & (kpos <= qpos_ref[...])
        fac = fac_ref[...]
        for h in range(heads):
            q = q_ref[:, h * DH:(h + 1) * DH]
            s = lax.dot_general(q, k, (((1,), (1,)), ((), ())),
                                preferred_element_type=jnp.float32)
            s = jnp.where(allowed, s * fac, -1e30)
            m_old = m_sc[h]
            m_new = jnp.maximum(m_old, jnp.max(s, axis=1, keepdims=True))
            alpha = jnp.exp(m_old - m_new)
            p = jnp.where(allowed, jnp.exp(s - m_new), 0.0)
            l_sc[h] = alpha * l_sc[h] + jnp.sum(p, axis=1, keepdims=True)
            pv = lax.dot_general(p.astype(jnp.bfloat16), v, (((1,), (0,)), ((), ())),
                                 preferred_element_type=jnp.float32)
            acc_sc[h] = alpha * acc_sc[h] + pv
            m_sc[h] = m_new

    @pl.when(j == steps - 1)
    def _():
        for h in range(heads):
            o_ref[:, h * DH:(h + 1) * DH] = (acc_sc[h] / l_sc[h]).astype(o_ref.dtype)


def attend(bounds, query_rows, kv, query_doc, query_pos, factor, key_doc, steps, bk):
    rows, width = query_rows.shape
    heads = width // DH

    def kv_map(j, b):
        return (jnp.minimum(b[0] + j, b[1]), 0)

    def kdoc_map(j, b):
        return (0, jnp.minimum(b[0] + j, b[1]))

    whole = lambda j, b: (0, 0)
    return pl.pallas_call(
        functools.partial(flash_kernel, heads=heads, bk=bk, steps=steps),
        out_shape=jax.ShapeDtypeStruct((rows, width), jnp.bfloat16),
        grid_spec=pltpu.PrefetchScalarGridSpec(
            num_scalar_prefetch=1,
            grid=(steps,),
            in_specs=[
                pl.BlockSpec((rows, width), whole),
                pl.BlockSpec((bk, 2 * DH), kv_map),
                pl.BlockSpec((rows, 1), whole),
                pl.BlockSpec((rows, 1), whole),
                pl.BlockSpec((rows, 1), whole),
                pl.BlockSpec((1, bk), kdoc_map),
            ],
            out_specs=pl.BlockSpec((rows, width), whole),
            scratch_shapes=[
                pltpu.VMEM((heads, rows, 1), jnp.float32),
                pltpu.VMEM((heads, rows, 1), jnp.float32),
                pltpu.VMEM((heads, rows, DH), jnp.float32),
            ],
        ),
        compiler_params=pltpu.CompilerParams(dimension_semantics=("arbitrary",)),
    )(bounds, query_rows, kv, query_doc, query_pos, factor, key_doc)


def body(queries, keys, values, doc_lengths):
    query_rows = queries[0]
    key_rows = keys[0]
    value_rows = values[0]
    lengths = doc_lengths[0]
    rows = query_rows.shape[0]
    cycle = lax.axis_size("ctx")
    count = rows * cycle
    base_len = count // 16
    position = lax.axis_index("ctx")
    first = position * rows
    ends = jnp.cumsum(lengths)
    starts = ends - lengths
    query_pos = first + jnp.arange(rows, dtype=jnp.int32)
    query_doc = doc_of(query_pos, ends)
    lookup = query_doc[:, None] == jnp.arange(DOCS, dtype=jnp.int32)[None, :]
    query_len = jnp.sum(jnp.where(lookup, lengths[None, :], 0), axis=1).astype(jnp.float32)
    factor = jnp.maximum(1.0, jnp.log(query_len) / math.log(float(base_len))) * (
        1.0 / math.sqrt(DH)
    )
    bk = min(BK, count)
    span = max(
        (c * rows + rows - 1) // bk - max(0, c * rows - (MOST - 1)) // bk + 1
        for c in range(cycle)
    )
    first_doc = jnp.sum((first >= ends).astype(jnp.int32))
    lo = jnp.sum(jnp.where(jnp.arange(DOCS) == first_doc, starts, 0)) // bk
    hi = (first + rows - 1) // bk
    bounds = jnp.stack([lo, hi]).astype(jnp.int32)
    kv_rows = jnp.concatenate([key_rows, value_rows], axis=1)
    kv = lax.all_gather(kv_rows, "ctx", axis=0, tiled=True)
    key_doc = doc_of(jnp.arange(count, dtype=jnp.int32), ends)[None, :]
    result = attend(
        bounds, query_rows, kv, query_doc[:, None], query_pos[:, None], factor[:, None],
        key_doc, span, bk,
    )
    own = lax.all_to_all(result, "mp", split_axis=0, concat_axis=1, tiled=True)
    moved = from_behind(own, "section", 1)
    return (own[None], moved[None])


def solution(mesh):
    return jax.shard_map(
        body,
        mesh=mesh,
        in_specs=(
            P("section", "ctx", "mp"),
            P("section", "ctx", "mp"),
            P("section", "ctx", "mp"),
            P("section", None),
        ),
        out_specs=(P("section", ("ctx", "mp"), None), P("section", ("ctx", "mp"), None)),
        check_vma=False,
    )
```

time: 209 us -> 149 us (0.71)
  the two profiles are of different devices: /device:TPU:128 before, /device:TPU:98 now
where the time goes in v1:
time: 149 us; the launch traced here: 147 us
  waiting for transfers between devices  71.2 us (48%)
  Pallas kernels  33.6 us (23%)
  between operations  16.6 us (11%)
  blocking collectives  13.6 us (9%)
  other arithmetic  7.17 us (5%)
  local copies, waits for them, and re-layouts  4.74 us (3%)
    all_gather x1, waiting for transfers between devices, body(): kv = lax.all_gather(kv_rows, 'ctx', axis=0, tiled=True)  58.3 us
    pallas_call x1, Pallas kernels, attend(): pl.pallas_call(functools.partial(flash_kernel, heads=heads, bk=bk, steps=...  33.6 us
    all_to_all x1, blocking collectives, body(): own = lax.all_to_all(result, 'mp', split_axis=0, concat_axis=1, tiled=True)  13.6 us
    ppermute x1, waiting for transfers between devices, from_behind(): return lax.ppermute(block, axis, route)  12.9 us
  transfers between devices with their start and end apart: 2, of which 2 were waited for; matrix products, arithmetic and copies ran while one was open for 6% of the time, Pallas kernels for 0%

profile of v1, /device:TPU:98, one launch (start us, length us, event | category | flops | bytes accessed | tf_op | source)
XLA Modules:
  0.0 147.0 jit_solution(2632332243969666494)
XLA Ops:
  7.2 0.0 all-gather.2.cloned.1.call-start
  7.2 1.5 %pad_maximum_fusion = bf16[256,256]{1,0:T(8,128)(2,1)} fusion(bf16[256,128]{1,0:T(8,128)(2,1)} %bitcast.23, bf16[256,128]{1,0:T(8,128)(2,1)} %bitcast.24), kind=kLoop, calls=%fused_computation.2 | loop fusion | flops 262144 | bytes 262144 | tf_op jit(solution)/shard_map/concatenate | solution.py:134
  8.8 0.0 all-gather.2.cloned.1.call-update
  8.8 0.7 copy.14
  9.6 0.1 reduce
  9.7 0.6 fusion
  10.3 1.9 %fusion.1 = s32[]{:T(128)} fusion(s32[16]{0:T(128)S(1)} %reduce, s32[]{:T(128)} %fusion, s32[1,16]{1,0:T(1,128)} %param.7), kind=kLoop, calls=%fused_computation.12 | loop fusion | flops 63 | bytes 136 | tf_op jit(solution)/shard_map/reduce_sum | solution.py:131
  14.8 0.1 convert_reduce_fusion.1
  14.8 0.7 select_reduce_fusion
  15.6 0.8 copy.16.fac_ref
  16.4 0.8 copy.15.qdoc_ref
  17.2 0.6 pad_add_fusion.bounds_ref
  17.8 0.6 iota_add_fusion.qpos_ref
  18.5 0.8 convert_reduce_fusion
  19.2 58.3 %all-gather.2.cloned.1.call-done.kv_ref = bf16[8192,256]{1,0:T(8,128)(2,1)} async-done(((bf16[256,256]{1,0:T(8,128)(2,1)}), bf16[8192,256]{1,0:T(8,128)(2,1)}) %all-gather.2.cloned.1.call-update) | async-done | bytes 4194320 | tf_op jit(solution)/shard_map/all_gather | solution.py:135
  77.5 33.6 %shard_map.59 = bf16[256,1024]{1,0:T(8,128)(2,1)} custom-call(s32[2]{0:T(128)} %pad_add_fusion.bounds_ref, bf16[256,1024]{1,0:T(8,128)(2,1)} %bitcast.19, bf16[8192,256]{1,0:T(8,128)(2,1)} %all-gather.2.cloned.1.call-done.kv_ref, s32[256,1]{1,0:T(8,128)} %copy.15.qdoc_ref, s32[256,1]{1,0:T(8,128)} %iota_add_fusion.qpos_ref, f32[256,1]{1,0:T(8,128)} %copy.16.fac_ref, ...), custom_call_target="tpu_custom_call" | custom-call | tf_op jit(solution)/shard_map/pallas_call | solution.py:80
  111.2 13.6 %all_to_all.19 = bf16[4,64,1024]{2,1,0:T(8,128)(2,1)S(1)} all-to-all(bf16[4,64,1024]{2,1,0:T(8,128)(2,1)} %bitcast.18), channel_id=1, replica_groups=mesh['section'=2,'ctx'=32,'mp'=4] {'mp'}, dimensions={0} | all-to-all | bytes 1048576 | tf_op jit(solution)/shard_map/all_to_all | solution.py:141
  124.8 0.1 collective-permute-start
  124.9 0.4 copy.17
  125.3 1.2 broadcast_in_dim.41
  126.5 12.9 %collective-permute-done = bf16[64,4096]{1,0:T(8,128)(2,1)S(1)} collective-permute-done((bf16[64,4096]{1,0:T(8,128)(2,1)S(1)}, bf16[64,4096]{1,0:T(8,128)(2,1)S(1)}, u32[]{:S(2)}, u32[]{:S(2)}) %collective-permute-start) | collective-permute-done | bytes 524320 | tf_op jit(solution)/shard_map/ppermute | solution.py:20
  139.4 0.8 copy.21
  (4 shorter events, 0.1 us)
Async XLA Ops:
  7.2 70.4 %all-gather.2.cloned.1.call-start = ((), (), s32[]{:S(2)}) async-start(), calls=%async_computation.1 | async-start | bytes 4325376 | tf_op jit(solution)/shard_map/all_gather | solution.py:135
  124.8 14.6 %collective-permute-start = (bf16[64,4096]{1,0:T(8,128)(2,1)S(1)}, bf16[64,4096]{1,0:T(8,128)(2,1)S(1)}, u32[]{:S(2)}, u32[]{:S(2)}) collective-permute-start(bf16[64,4096]{1,0:T(8,128)(2,1)S(1)} %bitcast.21), channel_id=1, source_target_pairs={{128,0},{0,128},{129,1},{1,129},{130,2},{2,130},{131,3},{3,131},{1... | collective-permute-start | bytes 1572872 | tf_op jit(solution)/shard_map/ppermute | solution.py:20
Sparse Core Ops, SparseCore 0:
  10.4 67.0 all-gather.1

commit v2 on v1

--- a/solution.py
+++ b/solution.py
@@ -37,28 +37,41 @@
         acc_sc[...] = jnp.zeros(acc_sc.shape, jnp.float32)
 
     blk = lo + j
+    full = bounds_ref[2 + j] == 1
 
-    @pl.when(blk <= hi)
-    def _():
+    def step(masked):
         k = kv_ref[:, :DH]
         v = kv_ref[:, DH:]
-        kpos = blk * bk + lax.broadcasted_iota(jnp.int32, (1, bk), 1)
-        allowed = (qdoc_ref[...] == kdoc_ref[...]) & (kpos <= qpos_ref[...])
+        if masked:
+            kpos = blk * bk + lax.broadcasted_iota(jnp.int32, (1, bk), 1)
+            allowed = (qdoc_ref[...] == kdoc_ref[...]) & (kpos <= qpos_ref[...])
         fac = fac_ref[...]
         for h in range(heads):
             q = q_ref[:, h * DH:(h + 1) * DH]
             s = lax.dot_general(q, k, (((1,), (1,)), ((), ())),
                                 preferred_element_type=jnp.float32)
-            s = jnp.where(allowed, s * fac, -1e30)
+            s = s * fac
+            if masked:
+                s = jnp.where(allowed, s, -1e30)
             m_old = m_sc[h]
             m_new = jnp.maximum(m_old, jnp.max(s, axis=1, keepdims=True))
             alpha = jnp.exp(m_old - m_new)
-            p = jnp.where(allowed, jnp.exp(s - m_new), 0.0)
+            p = jnp.exp(s - m_new)
+            if masked:
+                p = jnp.where(allowed, p, 0.0)
             l_sc[h] = alpha * l_sc[h] + jnp.sum(p, axis=1, keepdims=True)
             pv = lax.dot_general(p.astype(jnp.bfloat16), v, (((1,), (0,)), ((), ())),
                                  preferred_element_type=jnp.float32)
             acc_sc[h] = alpha * acc_sc[h] + pv
             m_sc[h] = m_new
+
+    @pl.when((blk <= hi) & full)
+    def _():
+        step(False)
+
+    @pl.when((blk <= hi) & jnp.logical_not(full))
+    def _():
+        step(True)
 
     @pl.when(j == steps - 1)
     def _():
@@ -130,7 +143,16 @@
     first_doc = jnp.sum((first >= ends).astype(jnp.int32))
     lo = jnp.sum(jnp.where(jnp.arange(DOCS) == first_doc, starts, 0)) // bk
     hi = (first + rows - 1) // bk
-    bounds = jnp.stack([lo, hi]).astype(jnp.int32)
+    last_doc = jnp.sum((first + rows - 1 >= ends).astype(jnp.int32))
+    block_first = jnp.minimum(lo + jnp.arange(span, dtype=jnp.int32), hi) * bk
+    block_last = block_first + bk - 1
+    full = (
+        (doc_of(block_first, ends) == first_doc)
+        & (doc_of(block_last, ends) == first_doc)
+        & (last_doc == first_doc)
+        & (block_last <= first)
+    )
+    bounds = jnp.concatenate([jnp.stack([lo, hi]), full.astype(jnp.int32)]).astype(jnp.int32)
     kv_rows = jnp.concatenate([key_rows, value_rows], axis=1)
     kv = lax.all_gather(kv_rows, "ctx", axis=0, tiled=True)
     key_doc = doc_of(jnp.arange(count, dtype=jnp.int32), ends)[None, :]

time: 149 us -> 149 us (level)
  the two profiles are of different devices: /device:TPU:98 before, /device:TPU:166 now
where the time goes in v2:
time: 149 us; the launch traced here: 150 us
  waiting for transfers between devices  67.6 us (45%)
  Pallas kernels  36.8 us (25%)
  between operations  17.8 us (12%)
  blocking collectives  15 us (10%)
  other arithmetic  7.97 us (5%)
  local copies, waits for them, and re-layouts  4.74 us (3%)
    all_gather x1, waiting for transfers between devices, body(): kv = lax.all_gather(kv_rows, 'ctx', axis=0, tiled=True)  54 us
    pallas_call x1, Pallas kernels, attend(): pl.pallas_call(functools.partial(flash_kernel, heads=heads, bk=bk, steps=...  36.8 us
    all_to_all x1, blocking collectives, body(): own = lax.all_to_all(result, 'mp', split_axis=0, concat_axis=1, tiled=True)  15 us
    ppermute x1, waiting for transfers between devices, from_behind(): return lax.ppermute(block, axis, route)  13.6 us
  transfers between devices with their start and end apart: 2, of which 2 were waited for; matrix products, arithmetic and copies ran while one was open for 7% of the time, Pallas kernels for 0%

profile of v2, /device:TPU:166, one launch (start us, length us, event | category | flops | bytes accessed | tf_op | source)
XLA Modules:
  0.0 150.1 jit_solution(14491059931779550229)
XLA Ops:
  7.2 0.0 all-gather.2.cloned.1.call-start
  7.2 1.5 %pad_maximum_fusion = bf16[256,256]{1,0:T(8,128)(2,1)} fusion(bf16[256,128]{1,0:T(8,128)(2,1)} %bitcast.23, bf16[256,128]{1,0:T(8,128)(2,1)} %bitcast.24), kind=kLoop, calls=%fused_computation.2 | loop fusion | flops 262144 | bytes 262144 | tf_op jit(solution)/shard_map/concatenate | solution.py:156
  8.8 0.0 all-gather.2.cloned.1.call-update
  8.8 0.7 copy.14
  9.6 0.1 reduce
  9.7 0.7 fusion
  10.3 1.9 %fusion.2 = (s32[]{:T(128)}, s32[]{:T(128)}) fusion(s32[16]{0:T(128)S(1)} %reduce, s32[]{:T(128)S(6)} %sub.21, s32[1,16]{1,0:T(1,128)} %param.7, s32[]{:T(128)} %fusion), kind=kLoop, calls=%fused_computation.17 | loop fusion | flops 110 | bytes 144 | tf_op jit(solution)/shard_map/reduce_sum | solution.py:146
  16.0 0.1 convert_reduce_fusion.1
  16.1 0.7 select_reduce_fusion
  16.8 0.8 copy.16.fac_ref
  17.6 0.8 copy.15.qdoc_ref
  18.4 0.2 convert_reduce_fusion.3
  18.6 0.6 and_convert_fusion
  19.3 0.6 pad_add_fusion.bounds_ref
  19.9 0.6 iota_add_fusion.qpos_ref
  20.5 0.8 convert_reduce_fusion
  21.3 54.0 %all-gather.2.cloned.1.call-done.kv_ref = bf16[8192,256]{1,0:T(8,128)(2,1)} async-done(((bf16[256,256]{1,0:T(8,128)(2,1)}), bf16[8192,256]{1,0:T(8,128)(2,1)}) %all-gather.2.cloned.1.call-update) | async-done | bytes 4194320 | tf_op jit(solution)/shard_map/all_gather | solution.py:157
  75.3 36.8 %shard_map.59 = bf16[256,1024]{1,0:T(8,128)(2,1)} custom-call(s32[11]{0:T(128)} %pad_add_fusion.bounds_ref, bf16[256,1024]{1,0:T(8,128)(2,1)} %bitcast.19, bf16[8192,256]{1,0:T(8,128)(2,1)} %all-gather.2.cloned.1.call-done.kv_ref, s32[256,1]{1,0:T(8,128)} %copy.15.qdoc_ref, s32[256,1]{1,0:T(8,128)} %iota_add_fusion.qpos_ref, f32[256,1]{1,0:T(8,128)} %copy.16.fac_ref, ...), custom_call_target="tpu_custom_call" | custom-call | tf_op jit(solution)/shard_map/pallas_call | solution.py:93
  112.1 15.0 %all_to_all.19 = bf16[4,64,1024]{2,1,0:T(8,128)(2,1)S(1)} all-to-all(bf16[4,64,1024]{2,1,0:T(8,128)(2,1)} %bitcast.18), channel_id=1, replica_groups=mesh['section'=2,'ctx'=32,'mp'=4] {'mp'}, dimensions={0} | all-to-all | bytes 1048576 | tf_op jit(solution)/shard_map/all_to_all | solution.py:163
  127.1 0.1 collective-permute-start
  127.2 0.4 copy.17
  127.6 1.2 broadcast_in_dim.45
  128.8 13.6 %collective-permute-done = bf16[64,4096]{1,0:T(8,128)(2,1)S(1)} collective-permute-done((bf16[64,4096]{1,0:T(8,128)(2,1)S(1)}, bf16[64,4096]{1,0:T(8,128)(2,1)S(1)}, u32[]{:S(2)}, u32[]{:S(2)}) %collective-permute-start) | collective-permute-done | bytes 524320 | tf_op jit(solution)/shard_map/ppermute | solution.py:20
  142.4 0.8 copy.21
  (5 shorter events, 0.1 us)
Async XLA Ops:
  7.2 68.1 %all-gather.2.cloned.1.call-start = ((), (), s32[]{:S(2)}) async-start(), calls=%async_computation.1 | async-start | bytes 4325376 | tf_op jit(solution)/shard_map/all_gather | solution.py:157
  127.1 15.3 %collective-permute-start = (bf16[64,4096]{1,0:T(8,128)(2,1)S(1)}, bf16[64,4096]{1,0:T(8,128)(2,1)S(1)}, u32[]{:S(2)}, u32[]{:S(2)}) collective-permute-start(bf16[64,4096]{1,0:T(8,128)(2,1)S(1)} %bitcast.21), channel_id=1, source_target_pairs={{128,0},{0,128},{129,1},{1,129},{130,2},{2,130},{131,3},{3,131},{1... | collective-permute-start | bytes 1572872 | tf_op jit(solution)/shard_map/ppermute | solution.py:20
Sparse Core Ops, SparseCore 0:
  10.4 64.8 all-gather.1

commit v3 on v2

--- a/solution.py
+++ b/solution.py
@@ -14,18 +14,12 @@
 BK = 512
 
 
-def from_behind(block, axis, distance):
-    devices = range(lax.axis_size(axis))
-    route = [((i - distance) % len(devices), i) for i in devices]
-    return lax.ppermute(block, axis, route)
-
-
 def doc_of(positions, ends):
     return jnp.sum((positions[:, None] >= ends[None, :]).astype(jnp.int32), axis=1)
 
 
-def flash_kernel(bounds_ref, q_ref, kv_ref, qdoc_ref, qpos_ref, fac_ref, kdoc_ref,
-                 o_ref, m_sc, l_sc, acc_sc, *, heads, bk, steps):
+def flash_kernel(bounds_ref, qt_ref, kv_ref, qdoc_ref, qpos_ref, fac_ref, kdoc_ref,
+                 o_ref, m_sc, l_sc, acc_sc, *, heads, rows, bk, steps):
     j = pl.program_id(0)
     lo = bounds_ref[0]
     hi = bounds_ref[1]
@@ -41,27 +35,25 @@
 
     def step(masked):
         k = kv_ref[:, :DH]
-        v = kv_ref[:, DH:]
+        vt = kv_ref[:, DH:].T
         if masked:
-            kpos = blk * bk + lax.broadcasted_iota(jnp.int32, (1, bk), 1)
-            allowed = (qdoc_ref[...] == kdoc_ref[...]) & (kpos <= qpos_ref[...])
+            kpos = blk * bk + lax.broadcasted_iota(jnp.int32, (bk, 1), 0)
+            allowed = (kdoc_ref[...] == qdoc_ref[...]) & (kpos <= qpos_ref[...])
         fac = fac_ref[...]
         for h in range(heads):
-            q = q_ref[:, h * DH:(h + 1) * DH]
-            s = lax.dot_general(q, k, (((1,), (1,)), ((), ())),
-                                preferred_element_type=jnp.float32)
+            cols = slice(h * rows, (h + 1) * rows)
+            s = jnp.dot(k, qt_ref[h], preferred_element_type=jnp.float32)
             s = s * fac
             if masked:
                 s = jnp.where(allowed, s, -1e30)
             m_old = m_sc[h]
-            m_new = jnp.maximum(m_old, jnp.max(s, axis=1, keepdims=True))
+            m_new = jnp.maximum(m_old, jnp.max(s, axis=0, keepdims=True))
             alpha = jnp.exp(m_old - m_new)
             p = jnp.exp(s - m_new)
             if masked:
                 p = jnp.where(allowed, p, 0.0)
-            l_sc[h] = alpha * l_sc[h] + jnp.sum(p, axis=1, keepdims=True)
-            pv = lax.dot_general(p.astype(jnp.bfloat16), v, (((1,), (0,)), ((), ())),
-                                 preferred_element_type=jnp.float32)
+            l_sc[h] = alpha * l_sc[h] + jnp.sum(p, axis=0, keepdims=True)
+            pv = jnp.dot(vt, p.astype(jnp.bfloat16), preferred_element_type=jnp.float32)
             acc_sc[h] = alpha * acc_sc[h] + pv
             m_sc[h] = m_new
 
@@ -76,43 +68,43 @@
     @pl.when(j == steps - 1)
     def _():
         for h in range(heads):
-            o_ref[:, h * DH:(h + 1) * DH] = (acc_sc[h] / l_sc[h]).astype(o_ref.dtype)
+            cols = slice(h * rows, (h + 1) * rows)
+            o_ref[:, h * DH:(h + 1) * DH] = (acc_sc[h] / l_sc[h]).T.astype(o_ref.dtype)
 
 
 def attend(bounds, query_rows, kv, query_doc, query_pos, factor, key_doc, steps, bk):
     rows, width = query_rows.shape
     heads = width // DH
+    qt = query_rows.reshape(rows, heads, DH).transpose(1, 2, 0)
 
     def kv_map(j, b):
         return (jnp.minimum(b[0] + j, b[1]), 0)
 
-    def kdoc_map(j, b):
-        return (0, jnp.minimum(b[0] + j, b[1]))
-
     whole = lambda j, b: (0, 0)
     return pl.pallas_call(
-        functools.partial(flash_kernel, heads=heads, bk=bk, steps=steps),
+        functools.partial(flash_kernel, heads=heads, rows=rows, bk=bk, steps=steps),
         out_shape=jax.ShapeDtypeStruct((rows, width), jnp.bfloat16),
         grid_spec=pltpu.PrefetchScalarGridSpec(
             num_scalar_prefetch=1,
             grid=(steps,),
             in_specs=[
-                pl.BlockSpec((rows, width), whole),
+                pl.BlockSpec((heads, DH, rows), lambda j, b: (0, 0, 0)),
                 pl.BlockSpec((bk, 2 * DH), kv_map),
-                pl.BlockSpec((rows, 1), whole),
-                pl.BlockSpec((rows, 1), whole),
-                pl.BlockSpec((rows, 1), whole),
-                pl.BlockSpec((1, bk), kdoc_map),
+                pl.BlockSpec((1, rows), whole),
+                pl.BlockSpec((1, rows), whole),
+                pl.BlockSpec((1, rows), whole),
+                pl.BlockSpec((bk, 1), kv_map),
             ],
             out_specs=pl.BlockSpec((rows, width), whole),
             scratch_shapes=[
-                pltpu.VMEM((heads, rows, 1), jnp.float32),
-                pltpu.VMEM((heads, rows, 1), jnp.float32),
-                pltpu.VMEM((heads, rows, DH), jnp.float32),
+                pltpu.VMEM((heads, 1, rows), jnp.float32),
+                pltpu.VMEM((heads, 1, rows), jnp.float32),
+                pltpu.VMEM((heads, DH, rows), jnp.float32),
             ],
         ),
         compiler_params=pltpu.CompilerParams(dimension_semantics=("arbitrary",)),
-    )(bounds, query_rows, kv, query_doc, query_pos, factor, key_doc)
+    )(bounds, qt, kv, query_doc.reshape(1, rows), query_pos.reshape(1, rows),
+      factor.reshape(1, rows), key_doc.reshape(-1, 1))
 
 
 def body(queries, keys, values, doc_lengths):
@@ -160,8 +152,18 @@
         bounds, query_rows, kv, query_doc[:, None], query_pos[:, None], factor[:, None],
         key_doc, span, bk,
     )
-    own = lax.all_to_all(result, "mp", split_axis=0, concat_axis=1, tiled=True)
-    moved = from_behind(own, "section", 1)
+    share = lax.axis_size("mp")
+    chunks = result.reshape(share, rows // share, result.shape[1])
+    sections = lax.axis_size("section")
+    got = lax.all_to_all(
+        jnp.concatenate([chunks] * sections, axis=0), ("section", "mp"), 0, 0, tiled=False
+    ).reshape(sections, share, rows // share, result.shape[1])
+    here = lax.axis_index("section")
+    behind = (here + sections - 1) % sections
+    own = jnp.take(got, here, axis=0)
+    moved = jnp.take(got, behind, axis=0)
+    own = own.transpose(1, 0, 2).reshape(rows // share, share * result.shape[1])
+    moved = moved.transpose(1, 0, 2).reshape(rows // share, share * result.shape[1])
     return (own[None], moved[None])
 
 

time: 149 us -> 145 us (0.973)
  the two profiles are of different devices: /device:TPU:166 before, /device:TPU:161 now
where the time goes in v3:
time: 145 us; the launch traced here: 146 us
  waiting for transfers between devices  68.6 us (47%)
  starting transfers between devices  25.1 us (17%)
  between operations  17.8 us (12%)
  Pallas kernels  17.2 us (12%)
  other arithmetic  10.2 us (7%)
  local copies, waits for them, and re-layouts  6.82 us (5%)
    all_gather x1, waiting for transfers between devices, body(): kv = lax.all_gather(kv_rows, 'ctx', axis=0, tiled=True)  53.9 us
    all_to_all x1, starting transfers between devices, body(): lax.all_to_all(jnp.concatenate([chunks] * sections, axis=0), ('section',...  25.1 us
    pallas_call x1, Pallas kernels, attend(): pl.pallas_call(functools.partial(flash_kernel, heads=heads, rows=rows, bk...  17.2 us
    all_to_all x1, waiting for transfers between devices, body(): lax.all_to_all(jnp.concatenate([chunks] * sections, axis=0), ('section',...  14.7 us
  transfers between devices with their start and end apart: 2, of which 2 were waited for; matrix products, arithmetic and copies ran while one was open for 7% of the time, Pallas kernels for 0%

profile of v3, /device:TPU:161, one launch (start us, length us, event | category | flops | bytes accessed | tf_op | source)
XLA Modules:
  0.0 145.7 jit_solution(12424671685710565971)
XLA Ops:
  7.2 0.0 copy-start.2
  7.2 0.0 copy-start
  7.2 0.0 all-gather.2.cloned.1.call-start
  7.2 1.6 %pad_maximum_fusion.1 = bf16[256,256]{1,0:T(8,128)(2,1)} fusion(bf16[256,128]{1,0:T(8,128)(2,1)} %bitcast.27, bf16[256,128]{1,0:T(8,128)(2,1)} %bitcast.28), kind=kLoop, calls=%fused_computation.7 | loop fusion | flops 262144 | bytes 262144 | tf_op jit(solution)/shard_map/concatenate | solution.py:148
  8.8 0.0 all-gather.2.cloned.1.call-update
  8.9 0.7 copy.15
  9.6 0.1 reduce
  9.7 0.6 fusion.2
  10.4 1.9 %fusion.4 = (s32[]{:T(128)}, s32[]{:T(128)}) fusion(s32[16]{0:T(128)S(1)} %reduce, s32[]{:T(128)S(6)} %sub.24, s32[1,16]{1,0:T(1,128)} %param.9, s32[]{:T(128)} %fusion.2), kind=kLoop, calls=%fused_computation.22 | loop fusion | flops 110 | bytes 144 | tf_op jit(solution)/shard_map/reduce_sum | solution.py:138
  15.9 0.2 convert_reduce_fusion
  16.1 2.7 %copy.17.kdoc_ref = s32[8192,1]{1,0:T(8,128)} copy(s32[8192,1]{0,1:T(1,128)S(1)} %bitcast.26) | data formatting | bytes 65536 | tf_op jit(solution)/shard_map/reshape;broadcast_in_dim | solution.py:107
  18.8 0.0 copy-done
  18.8 1.0 copy.16
  19.8 0.2 convert_reduce_fusion.3
  20.0 0.6 and_convert_fusion
  20.6 0.6 pad_add_fusion.bounds_ref
  21.2 0.5 iota_add_fusion.qpos_ref
  21.7 0.1 convert_reduce_fusion.1
  21.8 0.0 copy-start.1
  21.8 0.0 copy-done.2
  21.8 0.1 select_reduce_fusion
  21.9 0.5 maximum_multiply_fusion
  22.4 53.9 %all-gather.2.cloned.1.call-done.kv_ref = bf16[8192,256]{1,0:T(8,128)(2,1)} async-done(((bf16[256,256]{1,0:T(8,128)(2,1)}), bf16[8192,256]{1,0:T(8,128)(2,1)}) %all-gather.2.cloned.1.call-update) | async-done | bytes 4194320 | tf_op jit(solution)/shard_map/all_gather | solution.py:149
  76.3 0.0 copy-done.1
  76.3 17.2 %shard_map.59 = bf16[256,1024]{1,0:T(8,128)(2,1)} custom-call(s32[11]{0:T(128)} %pad_add_fusion.bounds_ref, bf16[8,128,256]{2,1,0:T(8,128)(2,1)} %bitcast.25, bf16[8192,256]{1,0:T(8,128)(2,1)} %all-gather.2.cloned.1.call-done.kv_ref, s32[1,256]{1,0:T(1,128)} %bitcast.29, s32[1,256]{1,0:T(1,128)} %iota_add_fusion.qpos_ref, f32[1,256]{1,0:T(1,128)} %bitcast.32, ...), custom_call_target="tpu_custom_call" | custom-call | tf_op jit(solution)/shard_map/pallas_call | solution.py:84
  93.5 2.3 %pad_maximum_fusion = bf16[8,64,1024]{2,1,0:T(8,128)(2,1)} fusion(bf16[4,64,1024]{2,1,0:T(8,128)(2,1)} %bitcast.24), kind=kLoop, calls=%fused_computation | loop fusion | flops 524288 | bytes 1572864 | tf_op jit(solution)/shard_map/concatenate | solution.py:159
  95.8 25.1 %all-to-all-start = ((bf16[8,64,1024]{2,1,0:T(8,128)(2,1)}), bf16[8,64,1024]{2,1,0:T(8,128)(2,1)S(1)}, u32[]{:S(2)}, u32[]{:S(2)}) async-start(bf16[8,64,1024]{2,1,0:T(8,128)(2,1)} %pad_maximum_fusion), calls=%async_computation | async-start | bytes 2097152 | tf_op jit(solution)/shard_map/all_to_all | solution.py:158
  120.8 14.7 %all-to-all-done = bf16[8,64,1024]{2,1,0:T(8,128)(2,1)S(1)} async-done(((bf16[8,64,1024]{2,1,0:T(8,128)(2,1)}), bf16[8,64,1024]{2,1,0:T(8,128)(2,1)S(1)}, u32[]{:S(2)}, u32[]{:S(2)}) %all-to-all-start) | async-done | bytes 1048608 | tf_op jit(solution)/shard_map/all_to_all | solution.py:158
  135.5 0.1 constant_dynamic-slice_fusion
  135.6 0.9 fusion
  136.5 1.2 broadcast_in_dim_reshape.6
  137.7 1.2 broadcast_in_dim_reshape.7
  (3 shorter events, 0.0 us)
Async XLA Ops:
  7.2 14.6 %copy-start.2 = (s32[1,16]{1,0:T(1,128)S(1)}, s32[1,16]{1,0:T(1,128)}, u32[]{:S(2)}) copy-start(s32[1,16]{1,0:T(1,128)} %param.9) | copy-start | bytes 196
  7.2 11.6 %copy-start = (bf16[1,256,1024]{2,1,0:T(8,128)(2,1)S(1)}, bf16[1,256,1024]{2,1,0:T(8,128)(2,1)}, u32[]{:S(2)}) copy-start(bf16[1,256,1024]{2,1,0:T(8,128)(2,1)} %param.6) | copy-start | bytes 1572868
  7.2 69.1 %all-gather.2.cloned.1.call-start = ((), (), s32[]{:S(2)}) async-start(), calls=%async_computation.1 | async-start | bytes 4325376 | tf_op jit(solution)/shard_map/all_gather | solution.py:149
  21.8 54.5 %copy-start.1 = (s32[256]{0:T(256)}, s32[256]{0:T(256)S(1)}, u32[]{:S(2)}) copy-start(s32[256]{0:T(256)S(1)} %convert_reduce_fusion.1) | copy-start | bytes 3076
  95.8 39.8 %all-to-all-start = ((bf16[8,64,1024]{2,1,0:T(8,128)(2,1)}), bf16[8,64,1024]{2,1,0:T(8,128)(2,1)S(1)}, u32[]{:S(2)}, u32[]{:S(2)}) async-start(bf16[8,64,1024]{2,1,0:T(8,128)(2,1)} %pad_maximum_fusion), calls=%async_computation | async-start | bytes 2097152 | tf_op jit(solution)/shard_map/all_to_all | solution.py:158
Sparse Core Ops, SparseCore 0:
  10.4 65.8 all-gather.1

commit v4 on v3

--- a/solution.py
+++ b/solution.py
@@ -36,26 +36,24 @@
     def step(masked):
         k = kv_ref[:, :DH]
         vt = kv_ref[:, DH:].T
+        fac = jnp.concatenate([fac_ref[...]] * heads, axis=1)
+        s = jnp.dot(k, qt_ref[...], preferred_element_type=jnp.float32)
+        s = s * fac
         if masked:
             kpos = blk * bk + lax.broadcasted_iota(jnp.int32, (bk, 1), 0)
             allowed = (kdoc_ref[...] == qdoc_ref[...]) & (kpos <= qpos_ref[...])
-        fac = fac_ref[...]
-        for h in range(heads):
-            cols = slice(h * rows, (h + 1) * rows)
-            s = jnp.dot(k, qt_ref[h], preferred_element_type=jnp.float32)
-            s = s * fac
-            if masked:
-                s = jnp.where(allowed, s, -1e30)
-            m_old = m_sc[h]
-            m_new = jnp.maximum(m_old, jnp.max(s, axis=0, keepdims=True))
-            alpha = jnp.exp(m_old - m_new)
-            p = jnp.exp(s - m_new)
-            if masked:
-                p = jnp.where(allowed, p, 0.0)
-            l_sc[h] = alpha * l_sc[h] + jnp.sum(p, axis=0, keepdims=True)
-            pv = jnp.dot(vt, p.astype(jnp.bfloat16), preferred_element_type=jnp.float32)
-            acc_sc[h] = alpha * acc_sc[h] + pv
-            m_sc[h] = m_new
+            allowed = jnp.concatenate([allowed] * heads, axis=1)
+            s = jnp.where(allowed, s, -1e30)
+        m_old = m_sc[...]
+        m_new = jnp.maximum(m_old, jnp.max(s, axis=0, keepdims=True))
+        alpha = jnp.exp(m_old - m_new)
+        p = jnp.exp(s - m_new)
+        if masked:
+            p = jnp.where(allowed, p, 0.0)
+        l_sc[...] = alpha * l_sc[...] + jnp.sum(p, axis=0, keepdims=True)
+        pv = jnp.dot(vt, p.astype(jnp.bfloat16), preferred_element_type=jnp.float32)
+        acc_sc[...] = alpha * acc_sc[...] + pv
+        m_sc[...] = m_new
 
     @pl.when((blk <= hi) & full)
     def _():
@@ -69,13 +67,13 @@
     def _():
         for h in range(heads):
             cols = slice(h * rows, (h + 1) * rows)
-            o_ref[:, h * DH:(h + 1) * DH] = (acc_sc[h] / l_sc[h]).T.astype(o_ref.dtype)
+            o_ref[:, h * DH:(h + 1) * DH] = (acc_sc[:, cols] / l_sc[:, cols]).T.astype(o_ref.dtype)
 
 
 def attend(bounds, query_rows, kv, query_doc, query_pos, factor, key_doc, steps, bk):
     rows, width = query_rows.shape
     heads = width // DH
-    qt = query_rows.reshape(rows, heads, DH).transpose(1, 2, 0)
+    qt = query_rows.reshape(rows, heads, DH).transpose(2, 1, 0).reshape(DH, heads * rows)
 
     def kv_map(j, b):
         return (jnp.minimum(b[0] + j, b[1]), 0)
@@ -88,7 +86,7 @@
             num_scalar_prefetch=1,
             grid=(steps,),
             in_specs=[
-                pl.BlockSpec((heads, DH, rows), lambda j, b: (0, 0, 0)),
+                pl.BlockSpec((DH, heads * rows), whole),
                 pl.BlockSpec((bk, 2 * DH), kv_map),
                 pl.BlockSpec((1, rows), whole),
                 pl.BlockSpec((1, rows), whole),
@@ -97,9 +95,9 @@
             ],
             out_specs=pl.BlockSpec((rows, width), whole),
             scratch_shapes=[
-                pltpu.VMEM((heads, 1, rows), jnp.float32),
-                pltpu.VMEM((heads, 1, rows), jnp.float32),
-                pltpu.VMEM((heads, DH, rows), jnp.float32),
+                pltpu.VMEM((1, heads * rows), jnp.float32),
+                pltpu.VMEM((1, heads * rows), jnp.float32),
+                pltpu.VMEM((DH, heads * rows), jnp.float32),
             ],
         ),
         compiler_params=pltpu.CompilerParams(dimension_semantics=("arbitrary",)),

time: 145 us -> 133 us (0.917)
  the two profiles are of different devices: /device:TPU:161 before, /device:TPU:160 now
where the time goes in v4:
time: 133 us; the launch traced here: 131 us
  waiting for transfers between devices  67.9 us (51%)
  starting transfers between devices  19.7 us (15%)
  between operations  17.8 us (13%)
  other arithmetic  10.2 us (8%)
  Pallas kernels  8 us (6%)
  local copies, waits for them, and re-layouts  7.39 us (6%)
    all_gather x1, waiting for transfers between devices, body(): kv = lax.all_gather(kv_rows, 'ctx', axis=0, tiled=True)  53 us
    all_to_all x1, starting transfers between devices, body(): lax.all_to_all(jnp.concatenate([chunks] * sections, axis=0), ('section',...  19.6 us
    all_to_all x1, waiting for transfers between devices, body(): lax.all_to_all(jnp.concatenate([chunks] * sections, axis=0), ('section',...  14.8 us
    pallas_call x1, Pallas kernels, attend(): pl.pallas_call(functools.partial(flash_kernel, heads=heads, rows=rows, bk...  8 us
    another operation x1, local copies, waits for them, and re-layouts, attend(): key_doc.reshape(-1, 1)  2.67 us
  transfers between devices with their start and end apart: 2, of which 2 were waited for; matrix products, arithmetic and copies ran while one was open for 8% of the time, Pallas kernels for 0%

profile of v4, /device:TPU:160, one launch (start us, length us, event | category | flops | bytes accessed | tf_op | source)
XLA Modules:
  0.0 131.0 jit_solution(18180518991831313)
XLA Ops:
  7.2 0.0 copy-start.2
  7.2 0.0 copy-start
  7.2 0.0 all-gather.2.cloned.1.call-start
  7.2 1.6 %pad_maximum_fusion.1 = bf16[256,256]{1,0:T(8,128)(2,1)} fusion(bf16[256,128]{1,0:T(8,128)(2,1)} %bitcast.33, bf16[256,128]{1,0:T(8,128)(2,1)} %bitcast.34), kind=kLoop, calls=%fused_computation.7 | loop fusion | flops 262144 | bytes 262144 | tf_op jit(solution)/shard_map/concatenate | solution.py:146
  8.8 0.0 all-gather.2.cloned.1.call-update
  8.9 0.7 copy.15
  9.6 0.1 reduce
  9.7 0.6 fusion.2
  10.4 1.9 %fusion.4 = (s32[]{:T(128)}, s32[]{:T(128)}) fusion(s32[16]{0:T(128)S(1)} %reduce, s32[]{:T(128)S(6)} %sub.24, s32[1,16]{1,0:T(1,128)} %param.9, s32[]{:T(128)} %fusion.2), kind=kLoop, calls=%fused_computation.22 | loop fusion | flops 110 | bytes 144 | tf_op jit(solution)/shard_map/reduce_sum | solution.py:136
  15.9 0.2 convert_reduce_fusion
  16.1 2.7 %copy.17.kdoc_ref = s32[8192,1]{1,0:T(8,128)} copy(s32[8192,1]{0,1:T(1,128)S(1)} %bitcast.32) | data formatting | bytes 65536 | tf_op jit(solution)/shard_map/reshape;broadcast_in_dim | solution.py:105
  18.8 0.0 copy-done
  18.8 0.1 copy.22
  18.9 0.6 copy.16
  19.5 0.9 copy.23
  20.4 0.2 convert_reduce_fusion.3
  20.6 0.6 and_convert_fusion
  21.1 0.6 pad_add_fusion.bounds_ref
  21.7 0.5 iota_add_fusion.qpos_ref
  22.3 0.1 convert_reduce_fusion.1
  22.4 0.0 copy-start.1
  22.4 0.0 copy-done.2
  22.4 0.1 select_reduce_fusion
  22.5 0.5 maximum_multiply_fusion
  23.0 53.0 %all-gather.2.cloned.1.call-done.kv_ref = bf16[8192,256]{1,0:T(8,128)(2,1)} async-done(((bf16[256,256]{1,0:T(8,128)(2,1)}), bf16[8192,256]{1,0:T(8,128)(2,1)}) %all-gather.2.cloned.1.call-update) | async-done | bytes 4194320 | tf_op jit(solution)/shard_map/all_gather | solution.py:147
  76.0 0.0 copy-done.1
  76.0 8.0 %shard_map.59 = bf16[256,1024]{1,0:T(8,128)(2,1)} custom-call(s32[11]{0:T(128)} %pad_add_fusion.bounds_ref, bf16[128,2048]{1,0:T(8,128)(2,1)} %bitcast.28, bf16[8192,256]{1,0:T(8,128)(2,1)} %all-gather.2.cloned.1.call-done.kv_ref, s32[1,256]{1,0:T(1,128)} %bitcast.35, s32[1,256]{1,0:T(1,128)} %iota_add_fusion.qpos_ref, f32[1,256]{1,0:T(1,128)} %bitcast.38, ...), custom_call_target="tpu_custom_call" | custom-call | tf_op jit(solution)/shard_map/pallas_call | solution.py:82
  84.0 2.3 %pad_maximum_fusion = bf16[8,64,1024]{2,1,0:T(8,128)(2,1)} fusion(bf16[4,64,1024]{2,1,0:T(8,128)(2,1)} %bitcast.27), kind=kLoop, calls=%fused_computation | loop fusion | flops 524288 | bytes 1572864 | tf_op jit(solution)/shard_map/concatenate | solution.py:157
  86.3 19.6 %all-to-all-start = ((bf16[8,64,1024]{2,1,0:T(8,128)(2,1)}), bf16[8,64,1024]{2,1,0:T(8,128)(2,1)S(1)}, u32[]{:S(2)}, u32[]{:S(2)}) async-start(bf16[8,64,1024]{2,1,0:T(8,128)(2,1)} %pad_maximum_fusion), calls=%async_computation | async-start | bytes 2097152 | tf_op jit(solution)/shard_map/all_to_all | solution.py:156
  106.0 14.8 %all-to-all-done = bf16[8,64,1024]{2,1,0:T(8,128)(2,1)S(1)} async-done(((bf16[8,64,1024]{2,1,0:T(8,128)(2,1)}), bf16[8,64,1024]{2,1,0:T(8,128)(2,1)S(1)}, u32[]{:S(2)}, u32[]{:S(2)}) %all-to-all-start) | async-done | bytes 1048608 | tf_op jit(solution)/shard_map/all_to_all | solution.py:156
  120.8 0.1 constant_dynamic-slice_fusion
  120.9 0.9 fusion
  121.8 1.2 broadcast_in_dim_reshape.6
  122.9 1.2 broadcast_in_dim_reshape.7
  (3 shorter events, 0.0 us)
Async XLA Ops:
  7.2 15.2 %copy-start.2 = (s32[1,16]{1,0:T(1,128)S(1)}, s32[1,16]{1,0:T(1,128)}, u32[]{:S(2)}) copy-start(s32[1,16]{1,0:T(1,128)} %param.9) | copy-start | bytes 196
  7.2 11.6 %copy-start = (bf16[1,256,1024]{2,1,0:T(8,128)(2,1)S(1)}, bf16[1,256,1024]{2,1,0:T(8,128)(2,1)}, u32[]{:S(2)}) copy-start(bf16[1,256,1024]{2,1,0:T(8,128)(2,1)} %param.6) | copy-start | bytes 1572868
  7.2 68.8 %all-gather.2.cloned.1.call-start = ((), (), s32[]{:S(2)}) async-start(), calls=%async_computation.1 | async-start | bytes 4325376 | tf_op jit(solution)/shard_map/all_gather | solution.py:147
  22.4 53.7 %copy-start.1 = (s32[256]{0:T(256)}, s32[256]{0:T(256)S(1)}, u32[]{:S(2)}) copy-start(s32[256]{0:T(256)S(1)} %convert_reduce_fusion.1) | copy-start | bytes 3076
  86.3 34.5 %all-to-all-start = ((bf16[8,64,1024]{2,1,0:T(8,128)(2,1)}), bf16[8,64,1024]{2,1,0:T(8,128)(2,1)S(1)}, u32[]{:S(2)}, u32[]{:S(2)}) async-start(bf16[8,64,1024]{2,1,0:T(8,128)(2,1)} %pad_maximum_fusion), calls=%async_computation | async-start | bytes 2097152 | tf_op jit(solution)/shard_map/all_to_all | solution.py:156
Sparse Core Ops, SparseCore 0:
  10.4 65.5 all-gather.1
